TPU v7x, 128 devices: a whole 4x4x4 slice. The times are simulated.
128 devices in a mesh: row: 8 (over y, core), col: 16 (over z, x).
Axes of the slice: x: 4, y: 4, z: 4, core: 2. Of those that a mesh axis runs over, the one named last changes fastest.
Arguments:
- fock: bfloat16 [32768, 16, 2048], P('row', 'col'), may hold values from -6 to 6
- lmo_coef: bfloat16 [32768, 1024], P(('row', 'col')), may hold values from -0.078125 to 0.078125
- three_index: bfloat16 [32768, 512], P(('row', 'col')), may hold values from -6 to 6
- rotation: bfloat16 [16, 8, 1024, 512], P('col', 'row'), may hold values from -0.1875 to 0.1875
- lmo_ids: int32 [16, 8], replicated, may hold values from 0 to 127, as said below
- domains: int32 [128, 8], replicated, may hold values from -1 to 255, as said below
Outputs:
- proj_fock: float32 [16, 8, 512, 512], P('col', 'row')
- three_rot: bfloat16 [16, 8, 512, 512], P('col', 'row')
Inputs may be any that keep to these rules, and one draw needn't show every extreme that they name: `lmo_ids`: every LMO number appears exactly once; row o lists the 8 LMOs owned by column set o. `domains`: entry k of a list is -1 or a block of row panel k; entry 0 is never -1. The present blocks of one list lie in distinct column sets. For one owner o and one entry k, the blocks of the lists of lmo_ids[o, j] over all j lie in distinct column sets; for one j and one entry k, those of lmo_ids[o, j] over all o do too.
All inputs are finite; a program needn't handle non-finite values.
Results may differ from a plain program's by a relative error of at most 0.02.
Values may be sent and summed in bfloat16 or wider, within the bound.
No kernel may reach another device: no remote copies, remote signals or barrier semaphores. Data moves between devices by JAX's collectives and lax.ppermute only.
A program may use at most 192 MiB of HBM per device.

v0:
```python
import jax
import jax.numpy as jnp
from jax import lax
from jax.sharding import PartitionSpec as P

BLK = 128
F32 = jnp.float32
BF16 = jnp.bfloat16


def pick(mask, table):
    return jnp.sum(jnp.where(mask, table, 0), axis=-1)


def body(fock, lmo_coef, three_index, rotation, lmo_ids, domains):
    num_sets = lax.axis_size("col")
    my_row = lax.axis_index("row")
    my_col = lax.axis_index("col")
    dev_rows = lmo_coef.shape[0]
    occ_width = lmo_coef.shape[1]
    dev_blocks = dev_rows // BLK
    dom_blocks = domains.shape[1]
    dom_width = dom_blocks * BLK
    panel_fock = fock[:, 0, :]
    panel_blocks = panel_fock.shape[0] // BLK
    col_blocks = panel_fock.shape[1] // BLK
    doms = jnp.take(domains, lmo_ids, axis=0)
    present = doms >= 0
    clipped = jnp.maximum(doms, 0)
    flat = clipped // dev_blocks
    cset = flat % num_sets
    sub = clipped % dev_blocks
    panel = flat // num_sets
    row_tile = cset * dev_blocks + sub
    col_tile = panel * dev_blocks + sub
    pres_k = lax.dynamic_index_in_dim(present, my_row, 2, keepdims=False)
    cset_k = lax.dynamic_index_in_dim(cset, my_row, 2, keepdims=False)
    sub_k = lax.dynamic_index_in_dim(sub, my_row, 2, keepdims=False)
    rtile_k = lax.dynamic_index_in_dim(row_tile, my_row, 2, keepdims=False)
    mine_k = pres_k & (cset_k == my_col)
    sub_o = pick(mine_k, sub_k)
    mine2 = present & (cset == my_col)
    ct = pick(mine2, col_tile)
    fock_tiles = panel_fock.reshape(panel_blocks, BLK, col_blocks, BLK)
    tiles_a = fock_tiles.at[rtile_k, :, ct, :].get(mode="promise_in_bounds")
    in_rows = jnp.concatenate([lmo_coef, three_index], axis=1).reshape(dev_blocks, BLK, -1)
    rows_a = jnp.take(in_rows, sub_o, axis=0, mode="clip")
    rows_a = lax.all_to_all(rows_a, "col", 0, 0, tiled=True)
    tiles_a, rows_a = lax.optimization_barrier((tiles_a, rows_a))
    tiles_a = lax.all_to_all(tiles_a, "col", 0, 0, tiled=True)
    gathered = lax.all_gather(lmo_coef, "row", axis=0, tiled=True)
    fock_lmo = jnp.dot(panel_fock, gathered, preferred_element_type=F32).astype(BF16)
    rows_a, tiles_a, fock_lmo = lax.optimization_barrier((rows_a, tiles_a, fock_lmo))
    coef_b = lax.psum_scatter(fock_lmo, "col", scatter_dimension=0, tiled=True)
    occ_term = jnp.einsum("ri,rj->ij", lmo_coef, coef_b, preferred_element_type=F32)
    occ_b = lax.psum(occ_term, ("row", "col")).astype(BF16)
    pres_o = lax.dynamic_index_in_dim(present, my_col, 0, keepdims=False)
    cset_o = lax.dynamic_index_in_dim(cset, my_col, 0, keepdims=False)
    pres_jk = lax.dynamic_index_in_dim(pres_o, my_row, 1, keepdims=False)
    cset_jk = lax.dynamic_index_in_dim(cset_o, my_row, 1, keepdims=False)
    rows_b = jnp.take(rows_a, cset_jk, axis=0, mode="clip")
    rows_b = jnp.where(pres_jk[:, None, None], rows_b, jnp.zeros_like(rows_b))
    slot_ids = jnp.broadcast_to(jnp.arange(dom_blocks, dtype=jnp.int32)[:, None], cset_o.shape)
    tiles_b = tiles_a.at[cset_o, slot_ids].get(mode="promise_in_bounds")
    live_b = pres_o & pres_jk[:, None]
    tiles_b = jnp.where(live_b[:, :, None, None], tiles_b, jnp.zeros_like(tiles_b))
    rows_dom, tiles_dom = (
        lax.all_to_all(rows_b, "row", 0, 0, tiled=True),
        lax.all_to_all(tiles_b, "row", 0, 0, tiled=True),
    )
    rows_dom = rows_dom.reshape(dom_width, -1)
    fc_a = jnp.take(coef_b.reshape(dev_blocks, BLK, occ_width), sub_o, axis=0, mode="clip")
    fc_a = lax.all_to_all(fc_a, "col", 0, 0, tiled=True)
    fc_a, occ_b, rows_dom, tiles_dom = lax.optimization_barrier((fc_a, occ_b, rows_dom, tiles_dom))
    fc_b = jnp.take(fc_a, cset_jk, axis=0, mode="clip")
    fc_b = jnp.where(pres_jk[:, None, None], fc_b, jnp.zeros_like(fc_b))
    fc_dom = lax.all_to_all(fc_b, "row", 0, 0, tiled=True).reshape(dom_width, occ_width)
    coef_dom = rows_dom[:, :occ_width]
    three_dom = rows_dom[:, occ_width:]
    correction = jnp.dot(coef_dom, occ_b, preferred_element_type=F32)
    proj_dom = (fc_dom.astype(F32) - 0.5 * correction).astype(BF16)
    slot_rot = rotation[0, 0]
    rot_tiles = slot_rot.reshape(dom_blocks, BLK, -1)
    fock_half = jnp.einsum("abtu,bun->atn", tiles_dom, rot_tiles, preferred_element_type=F32)
    fock_half = fock_half.reshape(dom_width, -1).astype(BF16)
    fock_rot = jnp.einsum("xm,xn->mn", slot_rot, fock_half, preferred_element_type=F32)
    coef_rot = jnp.einsum("xm,xi->mi", slot_rot, coef_dom, preferred_element_type=F32).astype(BF16)
    proj_rot = jnp.einsum("xm,xi->mi", slot_rot, proj_dom, preferred_element_type=F32).astype(BF16)
    proj_fock = fock_rot - jnp.einsum("mi,ni->mn", coef_rot, proj_rot, preferred_element_type=F32)
    proj_fock = proj_fock - jnp.einsum("mi,ni->mn", proj_rot, coef_rot, preferred_element_type=F32)
    three_rot = jnp.einsum("xm,xu->mu", slot_rot, three_dom, preferred_element_type=F32).astype(
        BF16
    )
    return (proj_fock[None, None], three_rot[None, None])


def solution(mesh):
    placed = (
        P("row", "col", None),
        P(("row", "col"), None),
        P(("row", "col"), None),
        P("col", "row", None, None),
        P(),
        P(),
    )
    return jax.shard_map(
        body,
        mesh=mesh,
        in_specs=placed,
        out_specs=(P("col", "row", None, None), P("col", "row", None, None)),
        check_vma=False,
    )
```

profile of v0, /device:TPU:1, one launch (start us, length us, event | category | flops | bytes accessed | tf_op | source)
XLA Modules:
  0.0 483.2 jit_solution(15179841917422128813)
XLA Ops:
  12.3 3.6 gather_fusion.2
  15.9 8.5 %all-to-all-start = ((bf16[16,128,1536]{2,1,0:T(8,128)(2,1)}), bf16[16,128,1536]{2,1,0:T(8,128)(2,1)}, u32[]{:S(2)}, u32[]{:S(2)}) async-start(bf16[16,128,1536]{2,1,0:T(8,128)(2,1)} %gather_fusion.2), calls=%async_computation | async-start | bytes 12582912 | tf_op jit(solution)/shard_map/all_to_all | solution.py:48
  24.4 9.7 %copy.44 = bf16[512,8,16,128]{3,2,1,0:T(8,128)(2,1)S(1)} copy(bf16[512,8,16,128]{3,1,2,0:T(8,128)(2,1)} %bitcast.68) | data formatting | bytes 33554432
  34.1 8.2 %copy.33 = bf16[32,128,16,128]{3,1,2,0:T(8,128)(2,1)} copy(bf16[32,128,16,128]{3,2,1,0:T(8,128)(2,1)S(1)} %bitcast.65) | data formatting | bytes 33554432 | tf_op jit(solution)/shard_map/reshape;squeeze | solution.py:44
  42.5 9.0 %gather_fusion.1 = bf16[128,128,128]{2,1,0:T(8,128)(2,1)} fusion(bf16[32,128,16,128]{3,1,2,0:T(8,128)(2,1)} %copy.33, s32[128]{0:T(128)S(1)} %reshape.121), kind=kCustom, calls=%fused_computation.1 | custom fusion | bytes 8389632 | tf_op jit(solution)/shard_map/gather | solution.py:45
  51.5 65.2 %all-to-all-done = bf16[16,128,1536]{2,1,0:T(8,128)(2,1)} async-done(((bf16[16,128,1536]{2,1,0:T(8,128)(2,1)}), bf16[16,128,1536]{2,1,0:T(8,128)(2,1)}, u32[]{:S(2)}, u32[]{:S(2)}) %all-to-all-start) | async-done | bytes 6291488 | tf_op jit(solution)/shard_map/all_to_all | solution.py:48
  116.7 5.4 %all-to-all-start.1 = ((bf16[16,8,128,128]{3,2,1,0:T(8,128)(2,1)}), bf16[16,8,128,128]{3,2,1,0:T(8,128)(2,1)}, u32[]{:S(2)}, u32[]{:S(2)}) async-start(bf16[16,8,128,128]{3,2,1,0:T(8,128)(2,1)} %bitcast.69), calls=%async_computation.1 | async-start | bytes 8388608 | tf_op jit(solution)/shard_map/all_to_all | solution.py:50
  122.2 23.4 %fusion.2 = bf16[4096,1024]{1,0:T(8,128)(2,1)} fusion(bf16[2048,1024]{1,0:T(8,128)(2,1)} %all-gather.2.cloned.1.call-done, bf16[4096,1,2048]{2,0,1:T(8,128)(2,1)} %param.6), kind=kOutput, calls=%fused_computation.9 | convolution fusion | flops 17184063488 | bytes 29360128 | tf_op jit(solution)/shard_map/dot_general | solution.py:52
  145.7 35.7 %all-to-all-done.1 = bf16[16,8,128,128]{3,2,1,0:T(8,128)(2,1)} async-done(((bf16[16,8,128,128]{3,2,1,0:T(8,128)(2,1)}), bf16[16,8,128,128]{3,2,1,0:T(8,128)(2,1)}, u32[]{:S(2)}, u32[]{:S(2)}) %all-to-all-start.1) | async-done | bytes 4194336 | tf_op jit(solution)/shard_map/all_to_all | solution.py:50
  182.2 3.2 gather_fusion.5
  185.4 2.8 copy_select_fusion
  188.2 7.4 %all-to-all-start.4 = ((bf16[8,8,128,128]{3,1,2,0:T(8,128)(2,1)}), bf16[8,8,128,128]{3,1,2,0:T(8,128)(2,1)S(1)}, u32[]{:S(2)}, u32[]{:S(2)}) async-start(bf16[8,8,128,128]{3,1,2,0:T(8,128)(2,1)} %copy_select_fusion), calls=%async_computation.5 | async-start | bytes 4194304 | tf_op jit(solution)/shard_map/all_to_all | solution.py:69
  195.8 5.4 %gather_fusion.4 = bf16[8,128,1536]{2,1,0:T(8,128)(2,1)} fusion(bf16[16,128,1536]{2,1,0:T(8,128)(2,1)} %all-to-all-done, s32[1024]{0:T(1024)S(1)} %pad_clamp_fusion), kind=kCustom, calls=%fused_computation.4 | custom fusion | bytes 6291488 | tf_op jit(solution)/shard_map/jit(_take)/gather | solution.py:61
  201.2 4.0 broadcast_select_fusion
  205.1 16.8 %all-to-all-done.4 = bf16[8,8,128,128]{3,1,2,0:T(8,128)(2,1)S(1)} async-done(((bf16[8,8,128,128]{3,1,2,0:T(8,128)(2,1)}), bf16[8,8,128,128]{3,1,2,0:T(8,128)(2,1)S(1)}, u32[]{:S(2)}, u32[]{:S(2)}) %all-to-all-start.4) | async-done | bytes 2097184 | tf_op jit(solution)/shard_map/all_to_all | solution.py:69
  223.2 5.2 %all-to-all-start.3 = ((bf16[8,128,1536]{2,1,0:T(8,128)(2,1)}), bf16[8,128,1536]{2,1,0:T(8,128)(2,1)}, u32[]{:S(2)}, u32[]{:S(2)}) async-start(bf16[8,128,1536]{2,1,0:T(8,128)(2,1)} %broadcast_select_fusion), calls=%async_computation.4 | async-start | bytes 6291456 | tf_op jit(solution)/shard_map/all_to_all | solution.py:68
  228.4 37.5 %reduce-scatter.2.cloned.1.call-done = bf16[256,1024]{1,0:T(8,128)(2,1)} async-done(((bf16[4096,1024]{1,0:T(8,128)(2,1)}), bf16[256,1024]{1,0:T(8,128)(2,1)}) %reduce-scatter.2.cloned.1.call-update) | async-done | bytes 524304 | tf_op jit(solution)/shard_map/reduce_scatter | solution.py:54
  266.0 3.8 gather_fusion.3
  269.8 4.9 %all-to-all-start.2 = ((bf16[16,128,1024]{2,1,0:T(8,128)(2,1)}), bf16[16,128,1024]{2,1,0:T(8,128)(2,1)}, u32[]{:S(2)}, u32[]{:S(2)}) async-start(bf16[16,128,1024]{2,1,0:T(8,128)(2,1)} %gather_fusion.3), calls=%async_computation.3 | async-start | bytes 8388608 | tf_op jit(solution)/shard_map/all_to_all | solution.py:73
  274.7 2.7 convolution_bitcast_fusion
  277.4 148.5 %all-reduce.1 = bf16[1024,1024]{0,1:T(8,128)(2,1)} all-reduce(f32[1024,1024]{0,1:T(8,128)} %convolution_bitcast_fusion), channel_id=1, replica_groups=mesh['row'=8,'col'=16] {'row','col'}, use_global_device_ids=true, to_apply=%region_3.4 | all-reduce | flops 1048576 | bytes 6291456 | tf_op jit(solution)/shard_map/psum | solution.py:56
  425.9 2.9 gather_fusion.6
  428.8 1.5 broadcast_select_fusion.1
  430.3 7.0 %all-to-all-start.5 = ((bf16[8,128,1024]{2,1,0:T(8,128)(2,1)}), bf16[8,128,1024]{2,1,0:T(8,128)(2,1)}, u32[]{:S(2)}, u32[]{:S(2)}) async-start(bf16[8,128,1024]{2,1,0:T(8,128)(2,1)} %broadcast_select_fusion.1), calls=%async_computation.6 | async-start | bytes 4194304 | tf_op jit(solution)/shard_map/all_to_all | solution.py:77
  437.4 2.0 fusion.17
  440.3 2.9 fusion.11
  443.2 4.3 convolution_bitcast_fusion.1
  447.6 16.3 %all-to-all-done.5 = bf16[8,128,1024]{2,1,0:T(8,128)(2,1)} async-done(((bf16[8,128,1024]{2,1,0:T(8,128)(2,1)}), bf16[8,128,1024]{2,1,0:T(8,128)(2,1)}, u32[]{:S(2)}, u32[]{:S(2)}) %all-to-all-start.5) | async-done | bytes 2097184 | tf_op jit(solution)/shard_map/all_to_all | solution.py:77
  463.8 6.3 %convolution_convert_fusion = bf16[1024,512]{1,0:T(8,128)(2,1)S(1)} fusion(bf16[1,1,1024,512]{3,2,1,0:T(8,128)(2,1)S(1)} %copy-done, bf16[1024,1024]{1,0:T(8,128)(2,1)} %bitcast.22, bf16[1024,1024]{0,1:T(8,128)(2,1)} %all-reduce.1, bf16[1024,1536]{1,0:T(8,128)(2,1)} %bitcast.7), kind=kOutput, calls=%fused_computation.23 | convolution fusion | flops 3225944064 | bytes 8388608 | tf_op jit(solution)/shard_map/xm,xi->mi/dot_general | solution.py:88
  471.1 2.0 convolution_subtract_fusion.1
  473.1 2.0 fusion.16
  475.1 1.3 copy.40
  (43 shorter events, 9.6 us)
Async XLA Ops:
  7.2 430.2 %copy-start = (bf16[1,1,1024,512]{3,2,1,0:T(8,128)(2,1)S(1)}, bf16[1,1,1024,512]{3,2,1,0:T(8,128)(2,1)}, u32[]{:S(2)}) copy-start(bf16[1,1,1024,512]{3,2,1,0:T(8,128)(2,1)} %param.9) | copy-start | bytes 3145732
  7.2 115.0 %all-gather.2.cloned.1.call-start = ((), (), s32[]{:S(2)}) async-start(), calls=%async_computation.7 | async-start | bytes 4718592 | tf_op jit(solution)/shard_map/all_gather | solution.py:51
  15.9 100.8 %all-to-all-start = ((bf16[16,128,1536]{2,1,0:T(8,128)(2,1)}), bf16[16,128,1536]{2,1,0:T(8,128)(2,1)}, u32[]{:S(2)}, u32[]{:S(2)}) async-start(bf16[16,128,1536]{2,1,0:T(8,128)(2,1)} %gather_fusion.2), calls=%async_computation | async-start | bytes 12582912 | tf_op jit(solution)/shard_map/all_to_all | solution.py:48
  116.7 64.7 %all-to-all-start.1 = ((bf16[16,8,128,128]{3,2,1,0:T(8,128)(2,1)}), bf16[16,8,128,128]{3,2,1,0:T(8,128)(2,1)}, u32[]{:S(2)}, u32[]{:S(2)}) async-start(bf16[16,8,128,128]{3,2,1,0:T(8,128)(2,1)} %bitcast.69), calls=%async_computation.1 | async-start | bytes 8388608 | tf_op jit(solution)/shard_map/all_to_all | solution.py:50
  122.1 143.8 %reduce-scatter.2.cloned.1.call-start = ((), (), s32[]{:S(2)}) async-start(), calls=%async_computation.8 | async-start | bytes 8912896 | tf_op jit(solution)/shard_map/reduce_scatter | solution.py:54
  188.2 33.8 %all-to-all-start.4 = ((bf16[8,8,128,128]{3,1,2,0:T(8,128)(2,1)}), bf16[8,8,128,128]{3,1,2,0:T(8,128)(2,1)S(1)}, u32[]{:S(2)}, u32[]{:S(2)}) async-start(bf16[8,8,128,128]{3,1,2,0:T(8,128)(2,1)} %copy_select_fusion), calls=%async_computation.5 | async-start | bytes 4194304 | tf_op jit(solution)/shard_map/all_to_all | solution.py:69
  221.9 1.3 copy-start.4
  223.2 46.6 %all-to-all-start.3 = ((bf16[8,128,1536]{2,1,0:T(8,128)(2,1)}), bf16[8,128,1536]{2,1,0:T(8,128)(2,1)}, u32[]{:S(2)}, u32[]{:S(2)}) async-start(bf16[8,128,1536]{2,1,0:T(8,128)(2,1)} %broadcast_select_fusion), calls=%async_computation.4 | async-start | bytes 6291456 | tf_op jit(solution)/shard_map/all_to_all | solution.py:68
  269.8 4.9 %copy-start.1 = (bf16[256,1024]{1,0:T(8,128)(2,1)S(1)}, bf16[256,1024]{1,0:T(8,128)(2,1)}, u32[]{:S(2)}) copy-start(bf16[256,1024]{1,0:T(8,128)(2,1)} %reduce-scatter.2.cloned.1.call-done) | copy-start | bytes 1572868
  269.8 4.9 %copy-start.2 = (bf16[256,1024]{1,0:T(8,128)(2,1)S(1)}, bf16[256,1024]{1,0:T(8,128)(2,1)}, u32[]{:S(2)}) copy-start(bf16[256,1024]{1,0:T(8,128)(2,1)} %param.7) | copy-start | bytes 1572868
  269.8 156.2 %all-to-all-start.2 = ((bf16[16,128,1024]{2,1,0:T(8,128)(2,1)}), bf16[16,128,1024]{2,1,0:T(8,128)(2,1)}, u32[]{:S(2)}, u32[]{:S(2)}) async-start(bf16[16,128,1024]{2,1,0:T(8,128)(2,1)} %gather_fusion.3), calls=%async_computation.3 | async-start | bytes 8388608 | tf_op jit(solution)/shard_map/all_to_all | solution.py:73
  430.3 33.5 %all-to-all-start.5 = ((bf16[8,128,1024]{2,1,0:T(8,128)(2,1)}), bf16[8,128,1024]{2,1,0:T(8,128)(2,1)}, u32[]{:S(2)}, u32[]{:S(2)}) async-start(bf16[8,128,1024]{2,1,0:T(8,128)(2,1)} %broadcast_select_fusion.1), calls=%async_computation.6 | async-start | bytes 4194304 | tf_op jit(solution)/shard_map/all_to_all | solution.py:77
  470.1 1.0 copy-start.3
Sparse Core Ops, SparseCore 0:
  9.7 35.7 all-gather.1
  181.5 84.3 reduce-scatter.1
where the time goes:
time: 484 us; the launch traced here: 483 us
  waiting for transfers between devices  172 us (36%)
  blocking collectives  149 us (31%)
  local copies, waits for them, and re-layouts  53 us (11%)
  matrix products  45.6 us (9%)
  starting transfers between devices  38.6 us (8%)
  between operations  14.2 us (3%)
  other arithmetic  11 us (2%)
    psum x1, blocking collectives, body(): occ_b = lax.psum(occ_term, ('row', 'col')).astype(BF16)  149 us
    all_to_all x1, waiting for transfers between devices, body(): rows_a = lax.all_to_all(rows_a, 'col', 0, 0, tiled=True)  65.2 us
    reduce_scatter x1, waiting for transfers between devices, body(): coef_b = lax.psum_scatter(fock_lmo, 'col', scatter_dimension=0, tiled=True)  37.5 us
    all_to_all x1, waiting for transfers between devices, body(): tiles_a = lax.all_to_all(tiles_a, 'col', 0, 0, tiled=True)  35.7 us
    dot_general x1, matrix products, body(): jnp.dot(panel_fock, gathered, preferred_element_type=F32).astype(BF16)  23.4 us
    all_to_all x1, waiting for transfers between devices, body(): lax.all_to_all(tiles_b, 'row', 0, 0, tiled=True)  16.8 us
    all_to_all x1, waiting for transfers between devices, body(): lax.all_to_all(fc_b, 'row', 0, 0, tiled=True).reshape(dom_width, occ_width)  16.3 us
    unnamed x14, local copies, waits for them, and re-layouts  15.1 us
  transfers between devices with their start and end apart: 8, of which 5 were waited for; matrix products, arithmetic and copies ran while one was open for 19% of the time, Pallas kernels for 0%

commit v1 on v0

--- a/solution.py
+++ b/solution.py
@@ -53,7 +53,7 @@
     rows_a, tiles_a, fock_lmo = lax.optimization_barrier((rows_a, tiles_a, fock_lmo))
     coef_b = lax.psum_scatter(fock_lmo, "col", scatter_dimension=0, tiled=True)
     occ_term = jnp.einsum("ri,rj->ij", lmo_coef, coef_b, preferred_element_type=F32)
-    occ_b = lax.psum(occ_term, ("row", "col")).astype(BF16)
+    occ_b = lax.psum(lax.psum(occ_term, "col"), "row").astype(BF16)
     pres_o = lax.dynamic_index_in_dim(present, my_col, 0, keepdims=False)
     cset_o = lax.dynamic_index_in_dim(cset, my_col, 0, keepdims=False)
     pres_jk = lax.dynamic_index_in_dim(pres_o, my_row, 1, keepdims=False)

time: 484 us -> 499 us (1.031)
  waiting for transfers between devices: 172 us -> 278 us
  blocking collectives: 149 us -> 58.8 us
    psum x1, blocking collectives: 149 us -> 58.8 us  [body(): occ_b = lax.psum(lax.psum(occ_term, 'col'), 'row').astype(BF16)]
    psum x0 -> x1, waiting for transfers between devices: none -> 85.6 us  [body(): occ_b = lax.psum(lax.psum(occ_term, 'col'), 'row').astype(BF16)]
    reduce_scatter x1, waiting for transfers between devices: 37.5 us -> 70.6 us  [body(): coef_b = lax.psum_scatter(fock_lmo, 'col', scatter_dimension=0, tiled=True)]
    all_to_all x1, waiting for transfers between devices: 16.8 us -> 0.01 us  [body(): lax.all_to_all(tiles_b, 'row', 0, 0, tiled=True)]
    unnamed x14 -> x12, local copies, waits for them, and re-layouts: 15.1 us -> 13.8 us
  transfers between devices with their start and end apart: 8 -> 9, of which waited for: 5 -> 6; matrix products, arithmetic and copies ran while one was open for 19% -> 18% of each run, Pallas kernels for 0% -> 0%
where the time goes in v1:
time: 499 us; the launch traced here: 498 us
  waiting for transfers between devices  278 us (56%)
  blocking collectives  58.8 us (12%)
  local copies, waits for them, and re-layouts  50.6 us (10%)
  matrix products  46.6 us (9%)
  starting transfers between devices  39.2 us (8%)
  between operations  13.9 us (3%)
  other arithmetic  10.9 us (2%)
    psum x1, waiting for transfers between devices, body(): occ_b = lax.psum(lax.psum(occ_term, 'col'), 'row').astype(BF16)  85.6 us
    reduce_scatter x1, waiting for transfers between devices, body(): coef_b = lax.psum_scatter(fock_lmo, 'col', scatter_dimension=0, tiled=True)  70.6 us
    all_to_all x1, waiting for transfers between devices, body(): rows_a = lax.all_to_all(rows_a, 'col', 0, 0, tiled=True)  65.2 us
    psum x1, blocking collectives, body(): occ_b = lax.psum(lax.psum(occ_term, 'col'), 'row').astype(BF16)  58.8 us
    all_to_all x1, waiting for transfers between devices, body(): tiles_a = lax.all_to_all(tiles_a, 'col', 0, 0, tiled=True)  35.8 us
    dot_general x1, matrix products, body(): jnp.dot(panel_fock, gathered, preferred_element_type=F32).astype(BF16)  23.4 us
    all_to_all x1, waiting for transfers between devices, body(): lax.all_to_all(fc_b, 'row', 0, 0, tiled=True).reshape(dom_width, occ_width)  16.2 us
    unnamed x12, local copies, waits for them, and re-layouts  13.8 us
  transfers between devices with their start and end apart: 9, of which 6 were waited for; matrix products, arithmetic and copies ran while one was open for 18% of the time, Pallas kernels for 0%

profile of v1, /device:TPU:1, one launch (start us, length us, event | category | flops | bytes accessed | tf_op | source)
XLA Modules:
  0.0 497.7 jit_solution(10488451801915459138)
XLA Ops:
  12.3 3.6 gather_fusion.2
  15.9 8.5 %all-to-all-start = ((bf16[16,128,1536]{2,1,0:T(8,128)(2,1)}), bf16[16,128,1536]{2,1,0:T(8,128)(2,1)}, u32[]{:S(2)}, u32[]{:S(2)}) async-start(bf16[16,128,1536]{2,1,0:T(8,128)(2,1)} %gather_fusion.2), calls=%async_computation | async-start | bytes 12582912 | tf_op jit(solution)/shard_map/all_to_all | solution.py:48
  24.4 9.7 %copy.44 = bf16[512,8,16,128]{3,2,1,0:T(8,128)(2,1)S(1)} copy(bf16[512,8,16,128]{3,1,2,0:T(8,128)(2,1)} %bitcast.68) | data formatting | bytes 33554432
  34.1 8.2 %copy.33 = bf16[32,128,16,128]{3,1,2,0:T(8,128)(2,1)} copy(bf16[32,128,16,128]{3,2,1,0:T(8,128)(2,1)S(1)} %bitcast.65) | data formatting | bytes 33554432 | tf_op jit(solution)/shard_map/reshape;squeeze | solution.py:44
  42.5 9.0 %gather_fusion.1 = bf16[128,128,128]{2,1,0:T(8,128)(2,1)} fusion(bf16[32,128,16,128]{3,1,2,0:T(8,128)(2,1)} %copy.33, s32[128]{0:T(128)S(1)} %reshape.121), kind=kCustom, calls=%fused_computation.1 | custom fusion | bytes 8389632 | tf_op jit(solution)/shard_map/gather | solution.py:45
  51.5 65.2 %all-to-all-done = bf16[16,128,1536]{2,1,0:T(8,128)(2,1)} async-done(((bf16[16,128,1536]{2,1,0:T(8,128)(2,1)}), bf16[16,128,1536]{2,1,0:T(8,128)(2,1)}, u32[]{:S(2)}, u32[]{:S(2)}) %all-to-all-start) | async-done | bytes 6291488 | tf_op jit(solution)/shard_map/all_to_all | solution.py:48
  116.7 5.4 %all-to-all-start.1 = ((bf16[16,8,128,128]{3,2,1,0:T(8,128)(2,1)}), bf16[16,8,128,128]{3,2,1,0:T(8,128)(2,1)}, u32[]{:S(2)}, u32[]{:S(2)}) async-start(bf16[16,8,128,128]{3,2,1,0:T(8,128)(2,1)} %bitcast.69), calls=%async_computation.1 | async-start | bytes 8388608 | tf_op jit(solution)/shard_map/all_to_all | solution.py:50
  122.2 23.4 %fusion.2 = bf16[4096,1024]{1,0:T(8,128)(2,1)} fusion(bf16[2048,1024]{1,0:T(8,128)(2,1)} %all-gather.2.cloned.1.call-done, bf16[4096,1,2048]{2,0,1:T(8,128)(2,1)} %param.6), kind=kOutput, calls=%fused_computation.9 | convolution fusion | flops 17184063488 | bytes 29360128 | tf_op jit(solution)/shard_map/dot_general | solution.py:52
  145.6 35.8 %all-to-all-done.1 = bf16[16,8,128,128]{3,2,1,0:T(8,128)(2,1)} async-done(((bf16[16,8,128,128]{3,2,1,0:T(8,128)(2,1)}), bf16[16,8,128,128]{3,2,1,0:T(8,128)(2,1)}, u32[]{:S(2)}, u32[]{:S(2)}) %all-to-all-start.1) | async-done | bytes 4194336 | tf_op jit(solution)/shard_map/all_to_all | solution.py:50
  182.2 3.2 gather_fusion.5
  185.4 2.7 copy_select_fusion
  188.1 7.6 %all-to-all-start.4 = ((bf16[8,8,128,128]{3,1,2,0:T(8,128)(2,1)}), bf16[8,8,128,128]{3,1,2,0:T(8,128)(2,1)}, u32[]{:S(2)}, u32[]{:S(2)}) async-start(bf16[8,8,128,128]{3,1,2,0:T(8,128)(2,1)} %copy_select_fusion), calls=%async_computation.5 | async-start | bytes 4194304 | tf_op jit(solution)/shard_map/all_to_all | solution.py:69
  195.7 70.6 %reduce-scatter.2.cloned.1.call-done = bf16[256,1024]{1,0:T(8,128)(2,1)} async-done(((bf16[4096,1024]{1,0:T(8,128)(2,1)}), bf16[256,1024]{1,0:T(8,128)(2,1)}) %reduce-scatter.2.cloned.1.call-update) | async-done | bytes 524304 | tf_op jit(solution)/shard_map/reduce_scatter | solution.py:54
  266.3 3.8 convolution_bitcast_fusion
  270.2 5.2 %gather_fusion.4 = bf16[8,128,1536]{2,1,0:T(8,128)(2,1)} fusion(bf16[16,128,1536]{2,1,0:T(8,128)(2,1)} %all-to-all-done, s32[1024]{0:T(1024)S(1)} %pad_clamp_fusion), kind=kCustom, calls=%fused_computation.4 | custom fusion | bytes 6291488 | tf_op jit(solution)/shard_map/jit(_take)/gather | solution.py:61
  275.5 3.9 broadcast_select_fusion
  279.4 6.2 %all-to-all-start.3 = ((bf16[8,128,1536]{2,1,0:T(8,128)(2,1)}), bf16[8,128,1536]{2,1,0:T(8,128)(2,1)}, u32[]{:S(2)}, u32[]{:S(2)}) async-start(bf16[8,128,1536]{2,1,0:T(8,128)(2,1)} %broadcast_select_fusion), calls=%async_computation.4 | async-start | bytes 6291456 | tf_op jit(solution)/shard_map/all_to_all | solution.py:68
  285.6 2.8 gather_fusion.3
  288.4 85.6 %all-reduce.3.cloned.1.call-done = f32[1024,1024]{0,1:T(8,128)} async-done(((f32[1024,1024]{0,1:T(8,128)}), f32[1024,1024]{0,1:T(8,128)}) %all-reduce.3.cloned.1.call-update) | async-done | bytes 4194320 | tf_op jit(solution)/shard_map/psum | solution.py:56
  374.0 5.3 %all-to-all-start.2 = ((bf16[16,128,1024]{2,1,0:T(8,128)(2,1)}), bf16[16,128,1024]{2,1,0:T(8,128)(2,1)}, u32[]{:S(2)}, u32[]{:S(2)}) async-start(bf16[16,128,1024]{2,1,0:T(8,128)(2,1)} %gather_fusion.3), calls=%async_computation.3 | async-start | bytes 8388608 | tf_op jit(solution)/shard_map/all_to_all | solution.py:73
  379.3 58.8 %all-reduce.4 = bf16[1024,1024]{0,1:T(8,128)(2,1)} all-reduce(f32[1024,1024]{0,1:T(8,128)} %all-reduce.3.cloned.1.call-done), channel_id=1, replica_groups=mesh['row'=8,'col'=16] {'row'}, use_global_device_ids=true, to_apply=%region_4.5 | all-reduce | flops 1048576 | bytes 6291456 | tf_op jit(solution)/shard_map/psum | solution.py:56
  438.1 3.5 all-to-all-done.2
  441.6 2.9 gather_fusion.6
  444.5 1.5 broadcast_select_fusion.1
  446.1 6.1 %all-to-all-start.5 = ((bf16[8,128,1024]{2,1,0:T(8,128)(2,1)}), bf16[8,128,1024]{2,1,0:T(8,128)(2,1)}, u32[]{:S(2)}, u32[]{:S(2)}) async-start(bf16[8,128,1024]{2,1,0:T(8,128)(2,1)} %broadcast_select_fusion.1), calls=%async_computation.6 | async-start | bytes 4194304 | tf_op jit(solution)/shard_map/all_to_all | solution.py:77
  452.2 2.0 fusion.17
  455.1 2.9 fusion.11
  458.0 4.4 convolution_bitcast_fusion.1
  462.4 16.2 %all-to-all-done.5 = bf16[8,128,1024]{2,1,0:T(8,128)(2,1)} async-done(((bf16[8,128,1024]{2,1,0:T(8,128)(2,1)}), bf16[8,128,1024]{2,1,0:T(8,128)(2,1)}, u32[]{:S(2)}, u32[]{:S(2)}) %all-to-all-start.5) | async-done | bytes 2097184 | tf_op jit(solution)/shard_map/all_to_all | solution.py:77
  478.6 6.3 %convolution_convert_fusion = bf16[1024,512]{1,0:T(8,128)(2,1)S(1)} fusion(bf16[1,1,1024,512]{3,2,1,0:T(8,128)(2,1)S(1)} %copy-done, bf16[1024,1024]{1,0:T(8,128)(2,1)} %bitcast.22, bf16[1024,1024]{0,1:T(8,128)(2,1)} %all-reduce.4, bf16[1024,1536]{1,0:T(8,128)(2,1)} %bitcast.7), kind=kOutput, calls=%fused_computation.23 | convolution fusion | flops 3225944064 | bytes 8388608 | tf_op jit(solution)/shard_map/xm,xi->mi/dot_general | solution.py:88
  485.9 2.0 convolution_subtract_fusion.1
  487.9 2.0 fusion.16
  (44 shorter events, 9.6 us)
Async XLA Ops:
  7.2 445.0 %copy-start = (bf16[1,1,1024,512]{3,2,1,0:T(8,128)(2,1)S(1)}, bf16[1,1,1024,512]{3,2,1,0:T(8,128)(2,1)}, u32[]{:S(2)}) copy-start(bf16[1,1,1024,512]{3,2,1,0:T(8,128)(2,1)} %param.9) | copy-start | bytes 3145732
  7.2 115.0 %all-gather.2.cloned.1.call-start = ((), (), s32[]{:S(2)}) async-start(), calls=%async_computation.7 | async-start | bytes 4718592 | tf_op jit(solution)/shard_map/all_gather | solution.py:51
  15.9 100.8 %all-to-all-start = ((bf16[16,128,1536]{2,1,0:T(8,128)(2,1)}), bf16[16,128,1536]{2,1,0:T(8,128)(2,1)}, u32[]{:S(2)}, u32[]{:S(2)}) async-start(bf16[16,128,1536]{2,1,0:T(8,128)(2,1)} %gather_fusion.2), calls=%async_computation | async-start | bytes 12582912 | tf_op jit(solution)/shard_map/all_to_all | solution.py:48
  116.7 64.7 %all-to-all-start.1 = ((bf16[16,8,128,128]{3,2,1,0:T(8,128)(2,1)}), bf16[16,8,128,128]{3,2,1,0:T(8,128)(2,1)}, u32[]{:S(2)}, u32[]{:S(2)}) async-start(bf16[16,8,128,128]{3,2,1,0:T(8,128)(2,1)} %bitcast.69), calls=%async_computation.1 | async-start | bytes 8388608 | tf_op jit(solution)/shard_map/all_to_all | solution.py:50
  122.1 144.1 %reduce-scatter.2.cloned.1.call-start = ((), (), s32[]{:S(2)}) async-start(), calls=%async_computation.8 | async-start | bytes 8912896 | tf_op jit(solution)/shard_map/reduce_scatter | solution.py:54
  188.1 78.2 %copy-start.2 = (bf16[256,1024]{1,0:T(8,128)(2,1)S(1)}, bf16[256,1024]{1,0:T(8,128)(2,1)}, u32[]{:S(2)}) copy-start(bf16[256,1024]{1,0:T(8,128)(2,1)} %param.7) | copy-start | bytes 1572868
  188.1 91.3 %all-to-all-start.4 = ((bf16[8,8,128,128]{3,1,2,0:T(8,128)(2,1)}), bf16[8,8,128,128]{3,1,2,0:T(8,128)(2,1)}, u32[]{:S(2)}, u32[]{:S(2)}) async-start(bf16[8,8,128,128]{3,1,2,0:T(8,128)(2,1)} %copy_select_fusion), calls=%async_computation.5 | async-start | bytes 4194304 | tf_op jit(solution)/shard_map/all_to_all | solution.py:69
  195.7 178.3 %all-reduce.3.cloned.1.call-start = ((), (), s32[]{:S(2)}) async-start(), calls=%async_computation.9 | async-start | bytes 8388608 | tf_op jit(solution)/shard_map/psum | solution.py:56
  279.3 6.3 %copy-start.1 = (bf16[256,1024]{1,0:T(8,128)(2,1)S(1)}, bf16[256,1024]{1,0:T(8,128)(2,1)}, u32[]{:S(2)}) copy-start(bf16[256,1024]{1,0:T(8,128)(2,1)} %reduce-scatter.2.cloned.1.call-done) | copy-start | bytes 1572868
  279.4 94.6 %all-to-all-start.3 = ((bf16[8,128,1536]{2,1,0:T(8,128)(2,1)}), bf16[8,128,1536]{2,1,0:T(8,128)(2,1)}, u32[]{:S(2)}, u32[]{:S(2)}) async-start(bf16[8,128,1536]{2,1,0:T(8,128)(2,1)} %broadcast_select_fusion), calls=%async_computation.4 | async-start | bytes 6291456 | tf_op jit(solution)/shard_map/all_to_all | solution.py:68
  374.0 67.7 %all-to-all-start.2 = ((bf16[16,128,1024]{2,1,0:T(8,128)(2,1)}), bf16[16,128,1024]{2,1,0:T(8,128)(2,1)}, u32[]{:S(2)}, u32[]{:S(2)}) async-start(bf16[16,128,1024]{2,1,0:T(8,128)(2,1)} %gather_fusion.3), calls=%async_computation.3 | async-start | bytes 8388608 | tf_op jit(solution)/shard_map/all_to_all | solution.py:73
  446.1 32.5 %all-to-all-start.5 = ((bf16[8,128,1024]{2,1,0:T(8,128)(2,1)}), bf16[8,128,1024]{2,1,0:T(8,128)(2,1)}, u32[]{:S(2)}, u32[]{:S(2)}) async-start(bf16[8,128,1024]{2,1,0:T(8,128)(2,1)} %broadcast_select_fusion.1), calls=%async_computation.6 | async-start | bytes 4194304 | tf_op jit(solution)/shard_map/all_to_all | solution.py:77
  484.9 1.0 copy-start.3
Sparse Core Ops, SparseCore 0:
  9.7 35.7 all-gather.1
  181.5 84.6 reduce-scatter.1
  270.2 103.7 all-reduce.2
